TPU v7x, 512 devices: a whole 4x8x8 slice. The times are simulated.
512 devices in a mesh: seq: 128 (over z, y, core), head: 4 (over x).
Axes of the slice: x: 4, y: 8, z: 8, core: 2. Of those that a mesh axis runs over, the one named last changes fastest.
Arguments:
- tokens: bfloat16 [16384, 4096], P('seq', 'head'), may hold values from -120 to 120
- shared_weight: bfloat16 [4096, 512], P(None, 'head'), may hold values from -0.75 to 0.75
- value_weight: bfloat16 [4096, 512], P(None, 'head'), may hold values from -0.09375 to 0.09375
- head_grad: bfloat16 [16384, 512], P('seq', 'head'), may hold values from -0.75 to 0.75
- sorted_slot: int32 [4, 16384], P('head', 'seq'), may hold values from 0 to 16383, as said below
Outputs:
- shared_grad: float32 [4096, 512], P('seq', 'head')
- value_grad: float32 [4096, 512], P('seq', 'head')
Inputs may be any that keep to these rules, and one draw needn't show every extreme that they name: For each head, sorted_slot[h] is a permutation of the positions. Of the 128 positions of one device (positions r * 128 to (r+1) * 128 - 1), at most 2 have sorted indices in the range s * 128 to (s+1) * 128 - 1 of one device s, for every head, and in every head some pair r, s reaches 2.
All inputs are finite; a program needn't handle non-finite values.
Results may differ from a plain program's by a relative error of at most 0.006.
The roundings to bfloat16 on the way count: a program that leaves them out, or rounds other values in their place, can miss the bound.
Values may be sent and summed in bfloat16 or wider, within the bound.
No kernel may reach another device: no remote copies, remote signals or barrier semaphores. Data moves between devices by JAX's collectives and lax.ppermute only.
A program may use at most 64 MiB of HBM per device.

v0:
```python
import math
import jax
import jax.numpy as jnp
from jax import lax
from jax.sharding import Mesh
from jax.sharding import PartitionSpec as P

GROUP = 64
SEQ = ("z", "y", "c")
eps_norm = 1e-06
masked_score = -1000000000.0


def shifted(value, axis, steps):
    count = lax.axis_size(axis)
    pairs = [(source, (source + steps) % count) for source in range(count)]
    return lax.ppermute(value, axis, pairs)


def unit_keys(block):
    block_float = block.astype(jnp.float32)
    norm_rows = jnp.sqrt(jnp.sum(block_float * block_float, axis=1, keepdims=True) + eps_norm)
    return (block_float / norm_rows).astype(jnp.bfloat16)


def per_device(tokens, shared_weight, value_weight, head_grad, sorted_slot):
    whole = lax.all_gather(tokens, "head", axis=1, tiled=True)
    tok_count = whole.shape[0]
    feat_count = whole.shape[1]
    head_width = shared_weight.shape[1]
    peer_count = lax.axis_size(SEQ)
    capacity = 2 * tok_count // peer_count
    group_count = tok_count // GROUP
    tail_start = tok_count - GROUP
    scale_factor = 1.0 / math.sqrt(head_width)
    query = jnp.dot(whole, shared_weight, preferred_element_type=jnp.float32).astype(jnp.bfloat16)
    values = jnp.dot(whole, value_weight, preferred_element_type=jnp.float32).astype(jnp.bfloat16)
    slot_ids = sorted_slot[0]
    target = slot_ids // tok_count
    local_slot = slot_ids - target * tok_count
    peer_ids = jnp.arange(peer_count, dtype=jnp.int32)
    row_ids = jnp.arange(tok_count, dtype=jnp.int32)
    earlier_rows = (row_ids[:, None] > row_ids[None, :]).astype(jnp.bfloat16)
    every_row = jnp.ones((tok_count,), dtype=bool)
    one_hot = ((target[:, None] == peer_ids[None, :]) & every_row[:, None]).astype(jnp.bfloat16)
    before = jnp.dot(earlier_rows, one_hot, preferred_element_type=jnp.float32)
    buffer_index = target * capacity + jnp.sum(before * one_hot.astype(jnp.float32), axis=1).astype(
        jnp.int32
    )
    payload = jnp.concatenate([query, values, head_grad], axis=1)
    send_rows = (
        jnp.zeros((peer_count * capacity, 3 * head_width), jnp.bfloat16)
        .at[buffer_index]
        .set(payload)
    )
    send_slots = (
        jnp.full((peer_count * capacity,), tok_count, jnp.int32).at[buffer_index].set(local_slot)
    )
    recv_rows, recv_slots = (
        lax.all_to_all(send_rows, SEQ, split_axis=0, concat_axis=0, tiled=True),
        lax.all_to_all(send_slots, SEQ, split_axis=0, concat_axis=0, tiled=True),
    )
    sorted_rows = (
        jnp.zeros((tok_count, 3 * head_width), jnp.bfloat16)
        .at[recv_slots]
        .set(recv_rows, mode="drop")
    )
    halo_rows = shifted(sorted_rows[tail_start:, : 2 * head_width], SEQ, 1)
    sorted_query = sorted_rows[:, :head_width]
    own_keys = unit_keys(sorted_query).reshape(group_count, GROUP, head_width)
    halo_keys = unit_keys(halo_rows[:, :head_width])
    q_blocks = sorted_query.reshape(group_count, GROUP, head_width)
    v_blocks = sorted_rows[:, head_width : 2 * head_width].reshape(group_count, GROUP, head_width)
    g_blocks = sorted_rows[:, 2 * head_width :].reshape(group_count, GROUP, head_width)
    prev_keys = jnp.concatenate([halo_keys[None], own_keys[:-1]], axis=0)
    prev_values = jnp.concatenate([halo_rows[None, :, head_width:], v_blocks[:-1]], axis=0)
    key_window = jnp.concatenate([own_keys, prev_keys], axis=1)
    value_window = jnp.concatenate([v_blocks, prev_values], axis=1)
    scores = (
        jnp.einsum("cqd,ckd->cqk", q_blocks, key_window, preferred_element_type=jnp.float32)
        * scale_factor
    )
    self_mask = jnp.arange(GROUP)[:, None] == jnp.arange(2 * GROUP)[None, :]
    scores = jnp.where(self_mask[None], masked_score, scores)
    probs = jax.nn.softmax(scores, axis=-1)
    dprob = jnp.einsum("cqd,ckd->cqk", g_blocks, value_window, preferred_element_type=jnp.float32)
    dscore = probs * (dprob - jnp.sum(probs * dprob, axis=-1, keepdims=True))
    probs_low = probs.astype(jnp.bfloat16)
    dscore_low = dscore.astype(jnp.bfloat16)
    dquery = (
        jnp.einsum("cqk,ckd->cqd", dscore_low, key_window, preferred_element_type=jnp.float32)
        * scale_factor
    )
    dkey_window = (
        jnp.einsum("cqk,cqd->ckd", dscore_low, q_blocks, preferred_element_type=jnp.float32)
        * scale_factor
    )
    dvalue_window = jnp.einsum(
        "cqk,cqd->ckd", probs_low, g_blocks, preferred_element_type=jnp.float32
    )
    grad_window = jnp.concatenate([dkey_window, dvalue_window], axis=-1)
    own_part = grad_window[:, :GROUP]
    later_part = grad_window[1:, GROUP:]
    outgoing = grad_window[0, GROUP:]
    incoming = shifted(outgoing, SEQ, -1)
    key_value = (own_part + jnp.concatenate([later_part, incoming[None]], axis=0)).reshape(
        tok_count, 2 * head_width
    )
    dquery_s = dquery.reshape(tok_count, head_width)
    dkey_s = key_value[:, :head_width]
    dvalue_s = key_value[:, head_width:]
    query_float = sorted_query.astype(jnp.float32)
    norm_s = jnp.sqrt(jnp.sum(query_float * query_float, axis=1, keepdims=True) + eps_norm)
    along = jnp.sum(query_float * dkey_s, axis=1, keepdims=True)
    dshared_s = dquery_s + dkey_s / norm_s - query_float * (along / norm_s**3)
    sorted_grads = jnp.concatenate(
        [dshared_s.astype(jnp.bfloat16), dvalue_s.astype(jnp.bfloat16)], axis=1
    )
    return_rows = sorted_grads[jnp.minimum(recv_slots, tok_count - 1)]
    back_rows = lax.all_to_all(return_rows, SEQ, split_axis=0, concat_axis=0, tiled=True)
    combined = back_rows[buffer_index]
    nz, ny, nc = (lax.axis_size(a) for a in SEQ)
    blocks = whole.reshape(tok_count, nz, ny, nc, feat_count // (nz * ny * nc))
    partial = jnp.einsum(
        "pzyck,ph->cyzkh", blocks, combined, preferred_element_type=jnp.float32
    ).reshape(feat_count, 2 * head_width)
    grads = partial
    for axis in ("c", "y", "z"):
        grads = lax.psum_scatter(grads, axis, scatter_dimension=0, tiled=True)
    return (grads[:, :head_width], grads[:, head_width:])


def split_mesh(mesh):
    devices = mesh.devices
    seq_n, head_n = devices.shape
    column = devices[:, 0]
    cores = sorted({d.core_on_chip for d in column})
    ys = sorted({d.coords[1] for d in column})
    nc, ny = (len(cores), len(ys))
    nz = seq_n // (nc * ny)
    grid = devices.reshape(nz, ny, nc, head_n)
    for z in range(nz):
        for y in range(ny):
            for c in range(nc):
                d = grid[z, y, c, 0]
                assert d.core_on_chip == cores[c] and d.coords[1] == ys[y]
    return Mesh(grid, SEQ + ("head",))


def solution(mesh):
    fine = split_mesh(mesh)
    in_specs = (P(SEQ, "head"), P(None, "head"), P(None, "head"), P(SEQ, "head"), P("head", SEQ))
    out_specs = (P(SEQ, "head"), P(SEQ, "head"))
    return jax.shard_map(
        per_device, mesh=fine, in_specs=in_specs, out_specs=out_specs, check_vma=False
    )
```

profile of v0, /device:TPU:2, one launch (start us, length us, event | category | flops | bytes accessed | tf_op | source)
XLA Modules:
  0.0 232.9 jit_solution(7353964962916671930)
XLA Ops:
  7.2 0.7 all-gather.2.cloned.1.call-update
  7.9 0.7 bitcast_subtract_fusion
  8.6 0.2 fusion.4
  8.8 0.7 fusion.32
  9.4 1.0 scatter_custom_fusion
  10.4 0.8 all_to_all.24
  11.2 17.8 %all-to-all-start = ((s32[128,2,1]{1,2,0:T(1,128)}), s32[128,2,1]{1,2,0:T(1,128)S(1)}, u32[]{:S(2)}, u32[]{:S(2)}) async-start(s32[128,2,1]{1,2,0:T(1,128)} %bitcast.4), calls=%async_computation | async-start | bytes 131072 | tf_op jit(solution)/shard_map/all_to_all | solution.py:61
  29.0 0.9 copy.16
  29.9 12.8 %all-gather.2.cloned.1.call-done = bf16[128,4096]{1,0:T(8,128)(2,1)} async-done(((bf16[128,1024]{1,0:T(8,128)(2,1)}), bf16[128,4096]{1,0:T(8,128)(2,1)}) %all-gather.2.cloned.1.call-update) | async-done | bytes 1048592 | tf_op jit(solution)/shard_map/all_gather | solution.py:27
  42.7 1.7 convolution_convert_fusion
  44.4 2.1 convolution_convert_fusion.1
  46.5 0.1 copy.17
  46.6 1.1 scatter_custom_fusion.1
  47.8 0.8 all_to_all.27
  48.5 14.9 %all-to-all-start.1 = ((bf16[128,2,384]{2,1,0:T(2,128)(2,1)}), bf16[128,2,384]{2,1,0:T(2,128)(2,1)S(1)}, u32[]{:S(2)}, u32[]{:S(2)}) async-start(bf16[128,2,384]{2,1,0:T(2,128)(2,1)} %all_to_all.27), calls=%async_computation.1 | async-start | bytes 393216 | tf_op jit(solution)/shard_map/all_to_all | solution.py:60
  63.4 0.5 broadcast.207
  63.9 0.8 reduce.3
  64.7 0.1 all_to_all.26
  64.9 11.9 %all-to-all-done.1 = bf16[128,2,384]{2,1,0:T(2,128)(2,1)S(1)} async-done(((bf16[128,2,384]{2,1,0:T(2,128)(2,1)}), bf16[128,2,384]{2,1,0:T(2,128)(2,1)S(1)}, u32[]{:S(2)}, u32[]{:S(2)}) %all-to-all-start.1) | async-done | bytes 196640 | tf_op jit(solution)/shard_map/all_to_all | solution.py:60
  76.9 1.5 scatter_custom_fusion.2
  78.4 0.1 fusion.11
  78.7 2.0 collective-permute-start
  80.7 6.5 %collective-permute-done = bf16[64,256]{1,0:T(8,128)(2,1)S(1)} collective-permute-done((bf16[64,256]{1,0:T(8,128)(2,1)S(1)}, bf16[64,256]{1,0:T(8,128)(2,1)S(1)}, u32[]{:S(2)}, u32[]{:S(2)}) %collective-permute-start) | collective-permute-done | bytes 32800 | tf_op jit(solution)/shard_map/ppermute | solution.py:17
  87.3 0.1 fusion.25
  87.4 0.1 fusion.30
  87.5 0.3 fusion.45
  87.8 0.4 fusion.27
  88.2 0.3 multiply_reduce_fusion
  88.5 0.1 multiply_convert_fusion
  88.6 0.2 convolution_multiply_fusion
  88.8 0.1 fusion.7
  88.9 1.9 collective-permute-start.1
  90.9 0.1 convolution_multiply_fusion.1
  91.0 2.4 %collective-permute-done.1 = f32[64,256]{0,1:T(8,128)S(1)} collective-permute-done((f32[64,256]{0,1:T(8,128)S(1)}, f32[64,256]{0,1:T(8,128)S(1)}, u32[]{:S(2)}, u32[]{:S(2)}) %collective-permute-start.1) | collective-permute-done | bytes 65568 | tf_op jit(solution)/shard_map/ppermute | solution.py:17
  93.4 0.1 copy.18
  93.5 0.1 fusion.13
  93.7 0.1 fusion.15
  93.8 1.2 gather_fusion
  94.9 0.7 all_to_all.30
  95.7 8.7 %all-to-all-start.2 = ((bf16[128,2,256]{2,1,0:T(2,128)(2,1)}), bf16[128,2,256]{2,1,0:T(2,128)(2,1)S(1)}, u32[]{:S(2)}, u32[]{:S(2)}) async-start(bf16[128,2,256]{2,1,0:T(2,128)(2,1)} %all_to_all.30), calls=%async_computation.2 | async-start | bytes 262144 | tf_op jit(solution)/shard_map/all_to_all | solution.py:120
  104.4 12.1 %all-to-all-done.2 = bf16[128,2,256]{2,1,0:T(2,128)(2,1)S(1)} async-done(((bf16[128,2,256]{2,1,0:T(2,128)(2,1)}), bf16[128,2,256]{2,1,0:T(2,128)(2,1)S(1)}, u32[]{:S(2)}, u32[]{:S(2)}) %all-to-all-start.2) | async-done | bytes 131104 | tf_op jit(solution)/shard_map/all_to_all | solution.py:120
  116.6 0.8 gather_fusion.1
  117.5 0.7 fusion.46
  118.2 2.2 copy.20
  120.5 12.8 %reduce-scatter.4.cloned.1.call-done = f32[2048,256]{1,0:T(8,128)} async-done(((f32[4096,256]{1,0:T(8,128)}), f32[2048,256]{1,0:T(8,128)}) %reduce-scatter.4.cloned.1.call-update) | async-done | bytes 2097168 | tf_op jit(solution)/shard_map/reduce_scatter | solution.py:129
  133.4 49.3 %reduce-scatter.6.cloned.1.call-done = f32[256,256]{1,0:T(8,128)} async-done(((f32[2048,256]{1,0:T(8,128)}), f32[256,256]{1,0:T(8,128)}) %reduce-scatter.6.cloned.1.call-update) | async-done | bytes 262160 | tf_op jit(solution)/shard_map/reduce_scatter | solution.py:129
  182.8 42.2 %reduce-scatter.8.cloned.1.call-done = f32[32,256]{1,0:T(8,128)} async-done(((f32[256,256]{1,0:T(8,128)}), f32[32,256]{1,0:T(8,128)}) %reduce-scatter.8.cloned.1.call-update) | async-done | bytes 32784 | tf_op jit(solution)/shard_map/reduce_scatter | solution.py:129
  225.0 1.3 fusion.44
  (31 shorter events, 0.6 us)
Async XLA Ops:
  7.2 35.5 %copy-start = (bf16[4096,128]{1,0:T(8,128)(2,1)S(1)}, bf16[4096,128]{1,0:T(8,128)(2,1)}, u32[]{:S(2)}) copy-start(bf16[4096,128]{1,0:T(8,128)(2,1)} %param.7) | copy-start | bytes 3145732
  7.2 35.5 %all-gather.2.cloned.1.call-start = ((), (), s32[]{:S(2)}) async-start(), calls=%async_computation.6 | async-start | bytes 1310720 | tf_op jit(solution)/shard_map/all_gather | solution.py:27
  11.2 37.4 %all-to-all-start = ((s32[128,2,1]{1,2,0:T(1,128)}), s32[128,2,1]{1,2,0:T(1,128)S(1)}, u32[]{:S(2)}, u32[]{:S(2)}) async-start(s32[128,2,1]{1,2,0:T(1,128)} %bitcast.4), calls=%async_computation | async-start | bytes 131072 | tf_op jit(solution)/shard_map/all_to_all | solution.py:61
  47.8 69.7 %copy-start.1 = (bf16[128,4096]{1,0:T(8,128)(2,1)S(1)}, bf16[128,4096]{1,0:T(8,128)(2,1)}, u32[]{:S(2)}) copy-start(bf16[128,4096]{1,0:T(8,128)(2,1)} %all-gather.2.cloned.1.call-done) | copy-start | bytes 3145732
  48.5 28.3 %all-to-all-start.1 = ((bf16[128,2,384]{2,1,0:T(2,128)(2,1)}), bf16[128,2,384]{2,1,0:T(2,128)(2,1)S(1)}, u32[]{:S(2)}, u32[]{:S(2)}) async-start(bf16[128,2,384]{2,1,0:T(2,128)(2,1)} %all_to_all.27), calls=%async_computation.1 | async-start | bytes 393216 | tf_op jit(solution)/shard_map/all_to_all | solution.py:60
  78.7 8.6 %collective-permute-start = (bf16[64,256]{1,0:T(8,128)(2,1)S(1)}, bf16[64,256]{1,0:T(8,128)(2,1)S(1)}, u32[]{:S(2)}, u32[]{:S(2)}) collective-permute-start(bf16[64,256]{1,0:T(8,128)(2,1)S(1)} %slice.75), channel_id=1, source_target_pairs={{0,4},{4,8},{8,12},{12,16},{16,20},{20,24},{24,28},{28,32},{32,36}... | collective-permute-start | bytes 98312 | tf_op jit(solution)/shard_map/ppermute | solution.py:17
  88.9 4.4 %collective-permute-start.1 = (f32[64,256]{0,1:T(8,128)S(1)}, f32[64,256]{0,1:T(8,128)S(1)}, u32[]{:S(2)}, u32[]{:S(2)}) collective-permute-start(f32[64,256]{0,1:T(8,128)S(1)} %get-tuple-element.5), channel_id=1, source_target_pairs={{0,508},{4,0},{8,4},{12,8},{16,12},{20,16},{24,20},{28,24},{32,28}... | collective-permute-start | bytes 196616 | tf_op jit(solution)/shard_map/ppermute | solution.py:17
  95.7 20.9 %all-to-all-start.2 = ((bf16[128,2,256]{2,1,0:T(2,128)(2,1)}), bf16[128,2,256]{2,1,0:T(2,128)(2,1)S(1)}, u32[]{:S(2)}, u32[]{:S(2)}) async-start(bf16[128,2,256]{2,1,0:T(2,128)(2,1)} %all_to_all.30), calls=%async_computation.2 | async-start | bytes 262144 | tf_op jit(solution)/shard_map/all_to_all | solution.py:120
  104.4 29.0 %reduce-scatter.4.cloned.1.call-start = ((), (), s32[]{:S(2)}) async-start(), calls=%async_computation.7 | async-start | bytes 6291456 | tf_op jit(solution)/shard_map/reduce_scatter | solution.py:129
  120.5 62.2 %reduce-scatter.6.cloned.1.call-start = ((), (), s32[]{:S(2)}) async-start(), calls=%async_computation.8 | async-start | bytes 2359296 | tf_op jit(solution)/shard_map/reduce_scatter | solution.py:129
  133.4 91.6 %reduce-scatter.8.cloned.1.call-start = ((), (), s32[]{:S(2)}) async-start(), calls=%async_computation.9 | async-start | bytes 294912 | tf_op jit(solution)/shard_map/reduce_scatter | solution.py:129
Sparse Core Ops, SparseCore 0:
  10.1 32.5 all-gather.1
  120.6 12.7 reduce-scatter.3
  136.2 46.4 reduce-scatter.5
  185.4 39.5 reduce-scatter.7
where the time goes:
time: 233 us
  waiting for transfers between devices  151 us (65%)
  starting transfers between devices  45.5 us (20%)
  between operations  14.1 us (6%)
  local copies, waits for them, and re-layouts  13.3 us (6%)
  matrix products  6.05 us (3%)
  other arithmetic  3.1 us (1%)
    reduce_scatter x3, waiting for transfers between devices, per_device(): grads = lax.psum_scatter(grads, axis, scatter_dimension=0, tiled=True)  104 us
    all_to_all x1, starting transfers between devices, per_device(): lax.all_to_all(send_slots, SEQ, split_axis=0, concat_axis=0, tiled=True)  17.8 us
    all_to_all x1, starting transfers between devices, per_device(): lax.all_to_all(send_rows, SEQ, split_axis=0, concat_axis=0, tiled=True)  14.9 us
    all_gather x1, waiting for transfers between devices, per_device(): whole = lax.all_gather(tokens, 'head', axis=1, tiled=True)  12.8 us
    all_to_all x1, waiting for transfers between devices, per_device(): lax.all_to_all(return_rows, SEQ, split_axis=0, concat_axis=0, tiled=True)  12.1 us
    all_to_all x1, waiting for transfers between devices, per_device(): lax.all_to_all(send_rows, SEQ, split_axis=0, concat_axis=0, tiled=True)  11.9 us
    ppermute x2, waiting for transfers between devices, shifted(): return lax.ppermute(value, axis, pairs)  8.87 us
    all_to_all x1, starting transfers between devices, per_device(): lax.all_to_all(return_rows, SEQ, split_axis=0, concat_axis=0, tiled=True)  8.7 us
  transfers between devices with their start and end apart: 9, of which 8 were waited for; matrix products, arithmetic and copies ran while one was open for 4% of the time, Pallas kernels for 0%

commit v1 on v0

--- a/solution.py
+++ b/solution.py
@@ -24,7 +24,10 @@
 
 
 def per_device(tokens, shared_weight, value_weight, head_grad, sorted_slot):
-    whole = lax.all_gather(tokens, "head", axis=1, tiled=True)
+    count_2 = lax.axis_size("head")
+    pieces = jnp.stack([tokens for _ in range(count_2)])
+    pieces = lax.all_to_all(pieces, "head", split_axis=0, concat_axis=0)
+    whole = jnp.concatenate(pieces, axis=1)
     tok_count = whole.shape[0]
     feat_count = whole.shape[1]
     head_width = shared_weight.shape[1]

time: 233 us -> 232 us (level)
  matrix products: 6.05 us -> 3.16 us
  local copies, waits for them, and re-layouts: 13.3 us -> 15.7 us
    all_gather x1 -> x0, waiting for transfers between devices: 12.8 us -> none  [per_device(): whole = lax.all_gather(tokens, 'head', axis=1, tiled=True)]
    all_to_all x0 -> x1, starting transfers between devices: none -> 9.36 us  [per_device(): pieces = lax.all_to_all(pieces, 'head', split_axis=0, concat_axis=0)]
    all_to_all x1, starting transfers between devices: 14.9 us -> 6.17 us  [per_device(): lax.all_to_all(send_rows, SEQ, split_axis=0, concat_axis=0, tiled=True)]
    all_to_all x1, waiting for transfers between devices: 0.01 us -> 8.17 us  [per_device(): lax.all_to_all(send_slots, SEQ, split_axis=0, concat_axis=0, tiled=True)]
    all_to_all x0 -> x1, waiting for transfers between devices: none -> 5.3 us  [per_device(): pieces = lax.all_to_all(pieces, 'head', split_axis=0, concat_axis=0)]
  transfers between devices with their start and end apart: 9 -> 9, of which waited for: 8 -> 9; matrix products, arithmetic and copies ran while one was open for 4% -> 3% of each run, Pallas kernels for 0% -> 0%
where the time goes in v1:
time: 232 us
  waiting for transfers between devices  150 us (65%)
  starting transfers between devices  45.8 us (20%)
  local copies, waits for them, and re-layouts  15.7 us (7%)
  between operations  14.1 us (6%)
  matrix products  3.16 us (1%)
  other arithmetic  3.11 us (1%)
    reduce_scatter x3, waiting for transfers between devices, per_device(): grads = lax.psum_scatter(grads, axis, scatter_dimension=0, tiled=True)  103 us
    all_to_all x1, starting transfers between devices, per_device(): lax.all_to_all(send_slots, SEQ, split_axis=0, concat_axis=0, tiled=True)  17.5 us
    all_to_all x1, waiting for transfers between devices, per_device(): lax.all_to_all(return_rows, SEQ, split_axis=0, concat_axis=0, tiled=True)  12.1 us
    all_to_all x1, waiting for transfers between devices, per_device(): lax.all_to_all(send_rows, SEQ, split_axis=0, concat_axis=0, tiled=True)  11.9 us
    all_to_all x1, starting transfers between devices, per_device(): pieces = lax.all_to_all(pieces, 'head', split_axis=0, concat_axis=0)  9.36 us
    ppermute x2, waiting for transfers between devices, shifted(): return lax.ppermute(value, axis, pairs)  8.87 us
    all_to_all x1, starting transfers between devices, per_device(): lax.all_to_all(return_rows, SEQ, split_axis=0, concat_axis=0, tiled=True)  8.7 us
    all_to_all x1, waiting for transfers between devices, per_device(): lax.all_to_all(send_slots, SEQ, split_axis=0, concat_axis=0, tiled=True)  8.17 us
  transfers between devices with their start and end apart: 9, of which 9 were waited for; matrix products, arithmetic and copies ran while one was open for 3% of the time, Pallas kernels for 0%

profile of v1, /device:TPU:2, one launch (start us, length us, event | category | flops | bytes accessed | tf_op | source)
XLA Modules:
  0.0 231.7 jit_solution(4067041207606551499)
XLA Ops:
  7.2 1.3 copy.16
  8.5 1.1 stack.2
  9.6 9.4 %all-to-all-start.1 = ((bf16[4,128,1024]{1,2,0:T(8,128)(2,1)}), bf16[4,128,1024]{1,2,0:T(8,128)(2,1)S(1)}, u32[]{:S(2)}, u32[]{:S(2)}) async-start(bf16[4,128,1024]{1,2,0:T(8,128)(2,1)} %stack.2), calls=%async_computation.1 | async-start | bytes 2097152 | tf_op jit(solution)/shard_map/all_to_all | solution.py:29
  19.0 0.9 copy.17
  19.8 0.7 bitcast_subtract_fusion
  20.5 0.2 fusion.4
  20.7 0.7 fusion.32
  21.3 1.0 scatter_custom_fusion
  22.3 0.8 all_to_all.27
  23.1 5.3 %all-to-all-done.1 = bf16[4,128,1024]{1,2,0:T(8,128)(2,1)S(1)} async-done(((bf16[4,128,1024]{1,2,0:T(8,128)(2,1)}), bf16[4,128,1024]{1,2,0:T(8,128)(2,1)S(1)}, u32[]{:S(2)}, u32[]{:S(2)}) %all-to-all-start.1) | async-done | bytes 1048608 | tf_op jit(solution)/shard_map/all_to_all | solution.py:29
  28.4 17.5 %all-to-all-start = ((s32[128,2,1]{1,2,0:T(1,128)}), s32[128,2,1]{1,2,0:T(1,128)S(1)}, u32[]{:S(2)}, u32[]{:S(2)}) async-start(s32[128,2,1]{1,2,0:T(1,128)} %bitcast.4), calls=%async_computation | async-start | bytes 131072 | tf_op jit(solution)/shard_map/all_to_all | solution.py:64
  45.9 0.5 convolution_convert_fusion
  46.4 0.5 convolution_convert_fusion.1
  46.9 0.1 copy.18
  47.0 1.1 scatter_custom_fusion.1
  48.1 0.7 all_to_all.31
  48.9 8.2 %all-to-all-done = s32[128,2,1]{1,2,0:T(1,128)S(1)} async-done(((s32[128,2,1]{1,2,0:T(1,128)}), s32[128,2,1]{1,2,0:T(1,128)S(1)}, u32[]{:S(2)}, u32[]{:S(2)}) %all-to-all-start) | async-done | bytes 1056 | tf_op jit(solution)/shard_map/all_to_all | solution.py:64
  57.0 6.2 %all-to-all-start.2 = ((bf16[128,2,384]{2,1,0:T(2,128)(2,1)}), bf16[128,2,384]{2,1,0:T(2,128)(2,1)S(1)}, u32[]{:S(2)}, u32[]{:S(2)}) async-start(bf16[128,2,384]{2,1,0:T(2,128)(2,1)} %all_to_all.31), calls=%async_computation.2 | async-start | bytes 393216 | tf_op jit(solution)/shard_map/all_to_all | solution.py:63
  63.2 0.5 broadcast.209
  63.7 0.8 reduce.3
  64.6 0.1 all_to_all.29
  64.7 11.9 %all-to-all-done.2 = bf16[128,2,384]{2,1,0:T(2,128)(2,1)S(1)} async-done(((bf16[128,2,384]{2,1,0:T(2,128)(2,1)}), bf16[128,2,384]{2,1,0:T(2,128)(2,1)S(1)}, u32[]{:S(2)}, u32[]{:S(2)}) %all-to-all-start.2) | async-done | bytes 196640 | tf_op jit(solution)/shard_map/all_to_all | solution.py:63
  76.8 1.5 scatter_custom_fusion.2
  78.5 2.0 collective-permute-start
  80.6 6.5 %collective-permute-done = bf16[64,256]{1,0:T(8,128)(2,1)S(1)} collective-permute-done((bf16[64,256]{1,0:T(8,128)(2,1)S(1)}, bf16[64,256]{1,0:T(8,128)(2,1)S(1)}, u32[]{:S(2)}, u32[]{:S(2)}) %collective-permute-start) | collective-permute-done | bytes 32800 | tf_op jit(solution)/shard_map/ppermute | solution.py:17
  87.3 0.3 fusion.45
  87.6 0.4 fusion.27
  88.0 0.3 multiply_reduce_fusion
  88.3 0.1 multiply_convert_fusion
  88.4 0.2 convolution_multiply_fusion
  88.6 0.1 fusion.7
  88.8 1.9 collective-permute-start.1
  90.7 0.1 convolution_multiply_fusion.1
  90.8 2.4 %collective-permute-done.1 = f32[64,256]{0,1:T(8,128)S(1)} collective-permute-done((f32[64,256]{0,1:T(8,128)S(1)}, f32[64,256]{0,1:T(8,128)S(1)}, u32[]{:S(2)}, u32[]{:S(2)}) %collective-permute-start.1) | collective-permute-done | bytes 65568 | tf_op jit(solution)/shard_map/ppermute | solution.py:17
  93.2 0.1 copy.19
  93.3 0.1 fusion.13
  93.5 0.1 fusion.15
  93.6 1.2 gather_fusion
  94.8 0.7 all_to_all.34
  95.5 8.7 %all-to-all-start.3 = ((bf16[128,2,256]{2,1,0:T(2,128)(2,1)}), bf16[128,2,256]{2,1,0:T(2,128)(2,1)S(1)}, u32[]{:S(2)}, u32[]{:S(2)}) async-start(bf16[128,2,256]{2,1,0:T(2,128)(2,1)} %all_to_all.34), calls=%async_computation.3 | async-start | bytes 262144 | tf_op jit(solution)/shard_map/all_to_all | solution.py:123
  104.2 12.1 %all-to-all-done.3 = bf16[128,2,256]{2,1,0:T(2,128)(2,1)S(1)} async-done(((bf16[128,2,256]{2,1,0:T(2,128)(2,1)}), bf16[128,2,256]{2,1,0:T(2,128)(2,1)S(1)}, u32[]{:S(2)}, u32[]{:S(2)}) %all-to-all-start.3) | async-done | bytes 131104 | tf_op jit(solution)/shard_map/all_to_all | solution.py:123
  116.4 0.8 gather_fusion.1
  117.3 0.7 fusion.46
  118.0 2.2 copy.20
  120.3 11.6 %reduce-scatter.4.cloned.1.call-done = f32[2048,256]{1,0:T(8,128)} async-done(((f32[4096,256]{1,0:T(8,128)}), f32[2048,256]{1,0:T(8,128)}) %reduce-scatter.4.cloned.1.call-update) | async-done | bytes 2097168 | tf_op jit(solution)/shard_map/reduce_scatter | solution.py:132
  132.0 49.2 %reduce-scatter.6.cloned.1.call-done = f32[256,256]{1,0:T(8,128)} async-done(((f32[2048,256]{1,0:T(8,128)}), f32[256,256]{1,0:T(8,128)}) %reduce-scatter.6.cloned.1.call-update) | async-done | bytes 262160 | tf_op jit(solution)/shard_map/reduce_scatter | solution.py:132
  181.3 42.6 %reduce-scatter.8.cloned.1.call-done = f32[32,256]{1,0:T(8,128)} async-done(((f32[256,256]{1,0:T(8,128)}), f32[32,256]{1,0:T(8,128)}) %reduce-scatter.8.cloned.1.call-update) | async-done | bytes 32784 | tf_op jit(solution)/shard_map/reduce_scatter | solution.py:132
  223.8 1.3 fusion.44
  (32 shorter events, 0.9 us)
Async XLA Ops:
  7.2 38.7 %copy-start = (bf16[4096,128]{1,0:T(8,128)(2,1)S(1)}, bf16[4096,128]{1,0:T(8,128)(2,1)}, u32[]{:S(2)}) copy-start(bf16[4096,128]{1,0:T(8,128)(2,1)} %param.7) | copy-start | bytes 3145732
  7.2 39.2 %copy-start.1 = (bf16[4096,128]{1,0:T(8,128)(2,1)S(1)}, bf16[4096,128]{1,0:T(8,128)(2,1)}, u32[]{:S(2)}) copy-start(bf16[4096,128]{1,0:T(8,128)(2,1)} %param.6) | copy-start | bytes 3145732
  9.6 18.8 %all-to-all-start.1 = ((bf16[4,128,1024]{1,2,0:T(8,128)(2,1)}), bf16[4,128,1024]{1,2,0:T(8,128)(2,1)S(1)}, u32[]{:S(2)}, u32[]{:S(2)}) async-start(bf16[4,128,1024]{1,2,0:T(8,128)(2,1)} %stack.2), calls=%async_computation.1 | async-start | bytes 2097152 | tf_op jit(solution)/shard_map/all_to_all | solution.py:29
  28.4 28.6 %all-to-all-start = ((s32[128,2,1]{1,2,0:T(1,128)}), s32[128,2,1]{1,2,0:T(1,128)S(1)}, u32[]{:S(2)}, u32[]{:S(2)}) async-start(s32[128,2,1]{1,2,0:T(1,128)} %bitcast.4), calls=%async_computation | async-start | bytes 131072 | tf_op jit(solution)/shard_map/all_to_all | solution.py:64
  57.0 19.6 %all-to-all-start.2 = ((bf16[128,2,384]{2,1,0:T(2,128)(2,1)}), bf16[128,2,384]{2,1,0:T(2,128)(2,1)S(1)}, u32[]{:S(2)}, u32[]{:S(2)}) async-start(bf16[128,2,384]{2,1,0:T(2,128)(2,1)} %all_to_all.31), calls=%async_computation.2 | async-start | bytes 393216 | tf_op jit(solution)/shard_map/all_to_all | solution.py:63
  78.5 8.6 %collective-permute-start = (bf16[64,256]{1,0:T(8,128)(2,1)S(1)}, bf16[64,256]{1,0:T(8,128)(2,1)S(1)}, u32[]{:S(2)}, u32[]{:S(2)}) collective-permute-start(bf16[64,256]{1,0:T(8,128)(2,1)S(1)} %slice.75), channel_id=1, source_target_pairs={{0,4},{4,8},{8,12},{12,16},{16,20},{20,24},{24,28},{28,32},{32,36}... | collective-permute-start | bytes 98312 | tf_op jit(solution)/shard_map/ppermute | solution.py:17
  88.8 4.4 %collective-permute-start.1 = (f32[64,256]{0,1:T(8,128)S(1)}, f32[64,256]{0,1:T(8,128)S(1)}, u32[]{:S(2)}, u32[]{:S(2)}) collective-permute-start(f32[64,256]{0,1:T(8,128)S(1)} %get-tuple-element.5), channel_id=1, source_target_pairs={{0,508},{4,0},{8,4},{12,8},{16,12},{20,16},{24,20},{28,24},{32,28}... | collective-permute-start | bytes 196616 | tf_op jit(solution)/shard_map/ppermute | solution.py:17
  95.5 20.9 %all-to-all-start.3 = ((bf16[128,2,256]{2,1,0:T(2,128)(2,1)}), bf16[128,2,256]{2,1,0:T(2,128)(2,1)S(1)}, u32[]{:S(2)}, u32[]{:S(2)}) async-start(bf16[128,2,256]{2,1,0:T(2,128)(2,1)} %all_to_all.34), calls=%async_computation.3 | async-start | bytes 262144 | tf_op jit(solution)/shard_map/all_to_all | solution.py:123
  104.2 27.8 %reduce-scatter.4.cloned.1.call-start = ((), (), s32[]{:S(2)}) async-start(), calls=%async_computation.7 | async-start | bytes 6291456 | tf_op jit(solution)/shard_map/reduce_scatter | solution.py:132
  120.3 61.0 %reduce-scatter.6.cloned.1.call-start = ((), (), s32[]{:S(2)}) async-start(), calls=%async_computation.8 | async-start | bytes 2359296 | tf_op jit(solution)/shard_map/reduce_scatter | solution.py:132
  132.0 91.9 %reduce-scatter.8.cloned.1.call-start = ((), (), s32[]{:S(2)}) async-start(), calls=%async_computation.9 | async-start | bytes 294912 | tf_op jit(solution)/shard_map/reduce_scatter | solution.py:132
Sparse Core Ops, SparseCore 0:
  120.4 11.5 reduce-scatter.3
  134.8 46.4 reduce-scatter.5
  184.0 39.7 reduce-scatter.7
